TPU v7x, 256 devices: a whole 4x4x8 slice. The times are simulated.
256 devices in a mesh: wide: 32 (over x, y, z_lo), narrow: 8 (over z_hi, core).
Axes of the slice: x: 4, y: 4, z: 8 (z_hi: 4, z_lo: 2; z = z_hi * 2 + z_lo), core: 2. Of those that a mesh axis runs over, the one named last changes fastest.
Arguments:
- r_matrix: bfloat16 [10240, 102400], P('narrow', 'wide'), may hold values from -0.01953125 to 0.01953125
- cmm_panel: bfloat16 [102400, 1280], P('wide', 'narrow'), may hold values from -18 to 18
- ctm_panel: bfloat16 [10240, 1280], P('narrow', 'wide'), may hold values from -18 to 18
- cee_in: float32 [10240, 10240], P('wide', 'narrow'), may hold values from -2 to 2
Outputs:
- cee_out: float32 [10240, 10240], P('wide', 'narrow')
All inputs are finite; a program needn't handle non-finite values.
Results may differ from a plain program's by a relative error of at most 0.0022.
Values may be sent and summed in bfloat16 or wider, within the bound.
No kernel may reach another device: no remote copies, remote signals or barrier semaphores. Data moves between devices by JAX's collectives and lax.ppermute only.
A program may use at most 128 MiB of HBM per device.

v0:
```python
import jax
import jax.numpy as jnp
from jax import lax
from jax.sharding import PartitionSpec as P


def spread(value, axis, root):
    mine = lax.axis_index(axis) == root
    return lax.psum(jnp.where(mine, value, jnp.zeros_like(value)), axis)


def per_device(r_matrix, cmm_panel, ctm_panel, cee_in):
    slope_rows = r_matrix.shape[0]
    tile_rows = cee_in.shape[0]
    panel_width = ctm_panel.shape[1]
    r_panel = r_matrix[:, :panel_width]
    z_part = jnp.dot(
        r_matrix,
        lax.all_gather(cmm_panel, "narrow", axis=1, tiled=True),
        preferred_element_type=jnp.float32,
    )
    z_mine = lax.psum_scatter(z_part, "wide", scatter_dimension=1, tiled=True)
    a_mine = (z_mine - ctm_panel.astype(jnp.float32)).astype(jnp.bfloat16)
    a_whole, r_whole, c_whole = (
        lax.all_gather(a_mine, "wide", axis=1, tiled=True),
        lax.all_gather(r_panel, "wide", axis=1, tiled=True),
        lax.all_gather(ctm_panel, "wide", axis=1, tiled=True),
    )
    wide_index = lax.axis_index("wide")
    narrow_index = lax.axis_index("narrow")
    owner = wide_index * tile_rows // slope_rows
    offset = jnp.clip(wide_index * tile_rows - narrow_index * slope_rows, 0, slope_rows - tile_rows)
    a_rows = lax.dynamic_slice_in_dim(a_whole, offset, tile_rows, 0)
    r_rows = lax.dynamic_slice_in_dim(r_whole, offset, tile_rows, 0)
    left_rows = jnp.concatenate([a_rows, r_rows], axis=1)
    left_rows = spread(left_rows, "narrow", owner)
    right_cols = jnp.concatenate([r_whole, -c_whole], axis=1)
    update = lax.dot_general(
        left_rows, right_cols, (((1,), (1,)), ((), ())), preferred_element_type=jnp.float32
    )
    return cee_in + update


def solution(mesh):
    placed = (P("narrow", "wide"), P("wide", "narrow"), P("narrow", "wide"), P("wide", "narrow"))
    return jax.shard_map(
        per_device, mesh=mesh, in_specs=placed, out_specs=P("wide", "narrow"), check_vma=False
    )
```

profile of v0, /device:TPU:14, one launch (start us, length us, event | category | flops | bytes accessed | tf_op | source)
XLA Modules:
  0.0 891.5 jit_solution(11240906440603850587)
XLA Ops:
  6.5 0.7 all-gather.5.cloned.1.call-update
  7.3 0.0 reduce-scatter.2.cloned.1.call-start
  7.3 83.2 %all-gather.5.cloned.1.call-done = bf16[3200,1280]{0,1:T(8,128)(2,1)} async-done(((bf16[3200,160]{0,1:T(8,128)(2,1)}), bf16[3200,1280]{0,1:T(8,128)(2,1)}) %all-gather.5.cloned.1.call-update) | async-done | bytes 8192016 | tf_op jit(solution)/shard_map/all_gather | solution.py:19
  90.5 17.7 %fusion.8 = f32[1280,1280]{0,1:T(8,128)} fusion(bf16[1280,3200]{1,0:T(8,128)(2,1)} %param.4, bf16[3200,1280]{0,1:T(8,128)(2,1)} %all-gather.5.cloned.1.call-done), kind=kOutput, calls=%fused_computation.10 | convolution fusion | flops 10485760000 | bytes 22937600 | tf_op jit(solution)/shard_map/dot_general | solution.py:17
  108.2 0.0 reduce-scatter.2.cloned.1.call-update
  108.3 0.0 all-gather.9.cloned.1.call-start
  108.3 0.9 slice-done
  109.2 0.8 copy.6
  110.0 0.0 all-gather.9.cloned.1.call-update
  110.0 0.0 all-gather.7.cloned.1.call-start
  110.1 179.7 %reduce-scatter.2.cloned.1.call-done = f32[1280,40]{0,1:T(8,128)} async-done(((f32[1280,1280]{0,1:T(8,128)}), f32[1280,40]{0,1:T(8,128)}) %reduce-scatter.2.cloned.1.call-update) | async-done | bytes 204816 | tf_op jit(solution)/shard_map/reduce_scatter | solution.py:22
  289.7 1.6 subtract_convert_fusion
  291.4 0.0 all-gather.11.cloned.1.call-start
  291.4 0.5 all-gather.11.cloned.1.call-update
  291.9 0.0 all-reduce.2.cloned.1.call-start
  292.0 165.5 %all-gather.9.cloned.1.call-done = bf16[1280,1280]{0,1:T(8,128)(2,1)} async-done(((bf16[1280,40]{0,1:T(8,128)(2,1)}), bf16[1280,1280]{0,1:T(8,128)(2,1)}) %all-gather.9.cloned.1.call-update) | async-done | bytes 3276816 | tf_op jit(solution)/shard_map/all_gather | solution.py:26
  457.5 1.6 constant_dynamic-slice_fusion
  459.1 163.1 %all-gather.7.cloned.1.call-done = bf16[1280,1280]{0,1:T(8,128)(2,1)} async-done(((bf16[1280,40]{0,1:T(8,128)(2,1)}), bf16[1280,1280]{0,1:T(8,128)(2,1)}) %all-gather.7.cloned.1.call-update) | async-done | bytes 3276816 | tf_op jit(solution)/shard_map/all_gather | solution.py:25
  622.2 1.6 constant_dynamic-slice_fusion.1
  623.8 1.8 maximum_select_fusion
  625.6 161.3 %all-gather.11.cloned.1.call-done = bf16[1280,1280]{0,1:T(8,128)(2,1)} async-done(((bf16[1280,40]{0,1:T(8,128)(2,1)}), bf16[1280,1280]{0,1:T(8,128)(2,1)}) %all-gather.11.cloned.1.call-update) | async-done | bytes 3276816 | tf_op jit(solution)/shard_map/all_gather | solution.py:27
  786.9 2.5 neg.3
  789.4 88.7 %all-reduce.2.cloned.1.call-done = bf16[320,2560]{0,1:T(8,128)(2,1)} async-done(((bf16[320,2560]{0,1:T(8,128)(2,1)}), bf16[320,2560]{0,1:T(8,128)(2,1)}) %all-reduce.2.cloned.1.call-update) | async-done | bytes 1638416 | tf_op jit(solution)/shard_map/psum | solution.py:9
  878.1 6.5 fusion.4
  (6 shorter events, 0.0 us)
Async XLA Ops:
  6.5 83.9 %all-gather.5.cloned.1.call-start = ((), (), s32[]{:S(2)}) async-start(), calls=%async_computation.1 | async-start | bytes 9216000 | tf_op jit(solution)/shard_map/all_gather | solution.py:19
  7.3 282.5 %reduce-scatter.2.cloned.1.call-start = ((), (), s32[]{:S(2)}) async-start(), calls=%async_computation.2 | async-start | bytes 6758400 | tf_op jit(solution)/shard_map/reduce_scatter | solution.py:22
  108.2 1.0 slice-start
  108.2 181.5 %copy-start = (bf16[1280,40]{0,1:T(8,128)(2,1)S(1)}, bf16[1280,40]{0,1:T(8,128)(2,1)}, u32[]{:S(2)}) copy-start(bf16[1280,40]{0,1:T(8,128)(2,1)} %param.6) | copy-start | bytes 307204
  108.3 349.3 %all-gather.9.cloned.1.call-start = ((), (), s32[]{:S(2)}) async-start(), calls=%async_computation.4 | async-start | bytes 3379200 | tf_op jit(solution)/shard_map/all_gather | solution.py:26
  110.0 512.2 %all-gather.7.cloned.1.call-start = ((), (), s32[]{:S(2)}) async-start(), calls=%async_computation.3 | async-start | bytes 3379200 | tf_op jit(solution)/shard_map/all_gather | solution.py:25
  291.4 495.5 %all-gather.11.cloned.1.call-start = ((), (), s32[]{:S(2)}) async-start(), calls=%async_computation.6 | async-start | bytes 3379200 | tf_op jit(solution)/shard_map/all_gather | solution.py:27
  291.9 586.2 %all-reduce.2.cloned.1.call-start = ((), (), s32[]{:S(2)}) async-start(), calls=%async_computation.5 | async-start | bytes 3932160 | tf_op jit(solution)/shard_map/psum | solution.py:9
Sparse Core Ops, SparseCore 0:
  9.2 81.2 all-gather.4
  108.4 181.3 reduce-scatter.1
  291.5 165.9 all-gather.8
  459.2 163.0 all-gather.6
  623.8 163.0 all-gather.10
  789.4 88.6 all-reduce.1
where the time goes:
time: 892 us; the launch traced here: 891 us
  waiting for transfers between devices  843 us (95%)
  matrix products  24.2 us (3%)
  between operations  13.5 us (2%)
    reduce_scatter x1, waiting for transfers between devices, per_device(): z_mine = lax.psum_scatter(z_part, 'wide', scatter_dimension=1, tiled=True)  180 us
    all_gather x1, waiting for transfers between devices, per_device(): lax.all_gather(r_panel, 'wide', axis=1, tiled=True)  165 us
    all_gather x1, waiting for transfers between devices, per_device(): lax.all_gather(a_mine, 'wide', axis=1, tiled=True)  163 us
    all_gather x1, waiting for transfers between devices, per_device(): lax.all_gather(ctm_panel, 'wide', axis=1, tiled=True)  161 us
    psum x1, waiting for transfers between devices, spread(): return lax.psum(jnp.where(mine, value, jnp.zeros_like(value)), axis)  88.7 us
    all_gather x1, waiting for transfers between devices, per_device(): lax.all_gather(cmm_panel, 'narrow', axis=1, tiled=True)  83.2 us
  transfers between devices with their start and end apart: 6, of which 6 were waited for; matrix products, arithmetic and copies ran while one was open for 1% of the time, Pallas kernels for 0%

commit v1 on v0

--- a/solution.py
+++ b/solution.py
@@ -22,7 +22,9 @@
     z_mine = lax.psum_scatter(z_part, "wide", scatter_dimension=1, tiled=True)
     a_mine = (z_mine - ctm_panel.astype(jnp.float32)).astype(jnp.bfloat16)
     a_whole, r_whole, c_whole = (
-        lax.all_gather(a_mine, "wide", axis=1, tiled=True),
+        jnp.concatenate(
+            lax.all_to_all(jnp.stack([a_mine] * lax.axis_size("wide")), "wide", 0, 0), axis=1
+        ),
         lax.all_gather(r_panel, "wide", axis=1, tiled=True),
         lax.all_gather(ctm_panel, "wide", axis=1, tiled=True),
     )

time: 892 us -> 737 us (0.83)
  waiting for transfers between devices: 843 us -> 667 us
  starting transfers between devices: 0.2 us -> 18.7 us
    all_gather x1 -> x0, waiting for transfers between devices: 163 us -> none  [per_device(): lax.all_gather(a_mine, 'wide', axis=1, tiled=True)]
    all_to_all x0 -> x1, starting transfers between devices: none -> 18.5 us  [per_device(): lax.all_to_all(jnp.stack([a_mine] * lax.axis_size('wide')), 'wide', 0, 0)]
    all_gather x1, waiting for transfers between devices: 165 us -> 152 us  [per_device(): lax.all_gather(r_panel, 'wide', axis=1, tiled=True)]
  transfers between devices with their start and end apart: 6 -> 6, of which waited for: 6 -> 5; matrix products, arithmetic and copies ran while one was open for 1% -> 2% of each run, Pallas kernels for 0% -> 0%
where the time goes in v1:
time: 737 us; the launch traced here: 736 us
  waiting for transfers between devices  667 us (91%)
  matrix products  24.2 us (3%)
  starting transfers between devices  18.7 us (3%)
  between operations  13.2 us (2%)
    reduce_scatter x1, waiting for transfers between devices, per_device(): z_mine = lax.psum_scatter(z_part, 'wide', scatter_dimension=1, tiled=True)  180 us
    all_gather x1, waiting for transfers between devices, per_device(): lax.all_gather(ctm_panel, 'wide', axis=1, tiled=True)  161 us
    all_gather x1, waiting for transfers between devices, per_device(): lax.all_gather(r_panel, 'wide', axis=1, tiled=True)  152 us
    psum x1, waiting for transfers between devices, spread(): return lax.psum(jnp.where(mine, value, jnp.zeros_like(value)), axis)  89.1 us
    all_gather x1, waiting for transfers between devices, per_device(): lax.all_gather(cmm_panel, 'narrow', axis=1, tiled=True)  83.2 us
    all_to_all x1, starting transfers between devices, per_device(): lax.all_to_all(jnp.stack([a_mine] * lax.axis_size('wide')), 'wide', 0, 0)  18.5 us
    dot_general x1, matrix products, per_device(): jnp.dot(r_matrix, lax.all_gather(cmm_panel, 'narrow', axis=1, tiled=True)...  17.7 us
  transfers between devices with their start and end apart: 6, of which 5 were waited for; matrix products, arithmetic and copies ran while one was open for 2% of the time, Pallas kernels for 0%

profile of v1, /device:TPU:14, one launch (start us, length us, event | category | flops | bytes accessed | tf_op | source)
XLA Modules:
  0.0 736.4 jit_solution(11738345147949729921)
XLA Ops:
  6.5 0.7 all-gather.4.cloned.1.call-update
  7.3 0.0 reduce-scatter.2.cloned.1.call-start
  7.3 83.2 %all-gather.4.cloned.1.call-done = bf16[3200,1280]{0,1:T(8,128)(2,1)} async-done(((bf16[3200,160]{0,1:T(8,128)(2,1)}), bf16[3200,1280]{0,1:T(8,128)(2,1)}) %all-gather.4.cloned.1.call-update) | async-done | bytes 8192016 | tf_op jit(solution)/shard_map/all_gather | solution.py:19
  90.5 17.7 %fusion.8 = f32[1280,1280]{0,1:T(8,128)} fusion(bf16[1280,3200]{1,0:T(8,128)(2,1)} %param.4, bf16[3200,1280]{0,1:T(8,128)(2,1)} %all-gather.4.cloned.1.call-done), kind=kOutput, calls=%fused_computation.10 | convolution fusion | flops 10485760000 | bytes 22937600 | tf_op jit(solution)/shard_map/dot_general | solution.py:17
  108.2 0.0 reduce-scatter.2.cloned.1.call-update
  108.3 0.0 all-gather.6.cloned.1.call-start
  108.3 0.9 slice-done
  109.2 0.8 copy.6
  110.0 180.3 %reduce-scatter.2.cloned.1.call-done = f32[1280,40]{0,1:T(8,128)} async-done(((f32[1280,1280]{0,1:T(8,128)}), f32[1280,40]{0,1:T(8,128)}) %reduce-scatter.2.cloned.1.call-update) | async-done | bytes 204816 | tf_op jit(solution)/shard_map/reduce_scatter | solution.py:22
  290.3 0.9 subtract_convert_fusion
  291.3 2.0 stack.2
  293.2 18.5 %all-to-all-start = ((bf16[32,1280,40]{1,2,0:T(8,128)(2,1)}), bf16[32,1280,40]{1,2,0:T(8,128)(2,1)S(1)}, u32[]{:S(2)}, u32[]{:S(2)}) async-start(bf16[32,1280,40]{1,2,0:T(8,128)(2,1)} %stack.2), calls=%async_computation.1 | async-start | bytes 6553600 | tf_op jit(solution)/shard_map/all_to_all | solution.py:26
  311.7 0.0 all-gather.8.cloned.1.call-start
  311.8 0.5 all-gather.8.cloned.1.call-update
  312.3 0.0 all-reduce.2.cloned.1.call-start
  312.4 152.3 %all-gather.6.cloned.1.call-done = bf16[1280,1280]{0,1:T(8,128)(2,1)} async-done(((bf16[1280,40]{0,1:T(8,128)(2,1)}), bf16[1280,1280]{0,1:T(8,128)(2,1)}) %all-gather.6.cloned.1.call-update) | async-done | bytes 3276816 | tf_op jit(solution)/shard_map/all_gather | solution.py:28
  464.7 2.5 constant_dynamic-slice_fusion
  467.2 0.4 constant_dynamic-slice_fusion.1
  467.6 3.0 maximum_select_fusion
  470.6 0.0 all-reduce.2.cloned.1.call-update
  470.6 161.2 %all-gather.8.cloned.1.call-done = bf16[1280,1280]{0,1:T(8,128)(2,1)} async-done(((bf16[1280,40]{0,1:T(8,128)(2,1)}), bf16[1280,1280]{0,1:T(8,128)(2,1)}) %all-gather.8.cloned.1.call-update) | async-done | bytes 3276816 | tf_op jit(solution)/shard_map/all_gather | solution.py:29
  631.7 2.5 neg.3
  634.3 89.1 %all-reduce.2.cloned.1.call-done = bf16[320,2560]{0,1:T(8,128)(2,1)} async-done(((bf16[320,2560]{0,1:T(8,128)(2,1)}), bf16[320,2560]{0,1:T(8,128)(2,1)}) %all-reduce.2.cloned.1.call-update) | async-done | bytes 1638416 | tf_op jit(solution)/shard_map/psum | solution.py:9
  723.4 6.5 fusion.4
  (6 shorter events, 0.0 us)
Async XLA Ops:
  6.5 83.9 %all-gather.4.cloned.1.call-start = ((), (), s32[]{:S(2)}) async-start(), calls=%async_computation.2 | async-start | bytes 9216000 | tf_op jit(solution)/shard_map/all_gather | solution.py:19
  7.3 283.1 %reduce-scatter.2.cloned.1.call-start = ((), (), s32[]{:S(2)}) async-start(), calls=%async_computation.3 | async-start | bytes 6758400 | tf_op jit(solution)/shard_map/reduce_scatter | solution.py:22
  108.2 1.0 slice-start
  108.2 182.1 %copy-start = (bf16[1280,40]{0,1:T(8,128)(2,1)S(1)}, bf16[1280,40]{0,1:T(8,128)(2,1)}, u32[]{:S(2)}) copy-start(bf16[1280,40]{0,1:T(8,128)(2,1)} %param.6) | copy-start | bytes 307204
  108.3 356.4 %all-gather.6.cloned.1.call-start = ((), (), s32[]{:S(2)}) async-start(), calls=%async_computation.4 | async-start | bytes 3379200 | tf_op jit(solution)/shard_map/all_gather | solution.py:28
  293.2 174.0 %all-to-all-start = ((bf16[32,1280,40]{1,2,0:T(8,128)(2,1)}), bf16[32,1280,40]{1,2,0:T(8,128)(2,1)S(1)}, u32[]{:S(2)}, u32[]{:S(2)}) async-start(bf16[32,1280,40]{1,2,0:T(8,128)(2,1)} %stack.2), calls=%async_computation.1 | async-start | bytes 6553600 | tf_op jit(solution)/shard_map/all_to_all | solution.py:26
  311.7 320.0 %all-gather.8.cloned.1.call-start = ((), (), s32[]{:S(2)}) async-start(), calls=%async_computation.6 | async-start | bytes 3379200 | tf_op jit(solution)/shard_map/all_gather | solution.py:29
  312.3 411.1 %all-reduce.2.cloned.1.call-start = ((), (), s32[]{:S(2)}) async-start(), calls=%async_computation.5 | async-start | bytes 3932160 | tf_op jit(solution)/shard_map/psum | solution.py:9
Sparse Core Ops, SparseCore 0:
  9.2 81.2 all-gather.3
  108.4 181.8 reduce-scatter.1
  292.1 172.5 all-gather.5
  466.3 165.3 all-gather.7
  634.3 89.0 all-reduce.1
